TPU v7x, 512 devices: a whole 4x8x8 slice. The times are simulated.
512 devices in a mesh: space: 32 (over y_lo, z), field: 16 (over x, y_hi, core).
Axes of the slice: x: 4, y: 8 (y_hi: 2, y_lo: 4; y = y_hi * 4 + y_lo), z: 8, core: 2. Of those that a mesh axis runs over, the one named last changes fastest.
Arguments:
- fields: float32 [16, 1024, 6144], P('field', 'space'), may hold values from -6 to 6
- zone_ids: int32 [1024, 6144], P('space'), may hold values from 0 to 7
- diffusivity: float32 [16, 8], P('field'), may hold values from 0.3 to 3
- heat_rate: float32 [15], replicated, may hold values from 0.3 to 1.5
- weight_in: bfloat16 [384, 16], replicated, may hold values from -1.5 to 1.5
- bias_in: float32 [384], replicated, may hold values from -3 to 3
- weight_mid: bfloat16 [384, 384], replicated, may hold values from -0.3125 to 0.3125
- bias_mid: float32 [384], replicated, may hold values from -3 to 3
- weight_out: bfloat16 [16, 384], replicated, may hold values from -0.3125 to 0.3125
- bias_out: float32 [16], replicated, may hold values from -2 to 2
Outputs:
- new_fields: float32 [16, 1024, 6144], P('field', 'space')
All inputs are finite; a program needn't handle non-finite values.
Results may differ from a plain program's by a relative error of at most 0.005.
Values may be sent and summed in bfloat16 or wider, within the bound.
No kernel may reach another device: no remote copies, remote signals or barrier semaphores. Data moves between devices by JAX's collectives and lax.ppermute only.
A program may use at most 64 MiB of HBM per device.

v0:
```python
import jax
import jax.numpy as jnp
from jax import lax
from jax.sharding import PartitionSpec as P

FIELDS = 16
SWEEPS = 3
ROWS_BLK = 1024
RELAX_WEIGHTS = (0.8, 1.25, 0.95)


def extended(cells, sides, width):
    for axis, dim in sides:
        count = lax.axis_size(axis)
        ends = count - 1
        head = lax.slice_in_dim(cells, 0, width, axis=dim)
        tail = lax.slice_in_dim(cells, cells.shape[dim] - width, cells.shape[dim], axis=dim)
        cells = jnp.concatenate(
            [
                lax.ppermute(tail, axis, [(i, (i + 1) % count) for i in range(ends)]),
                cells,
                lax.ppermute(head, axis, [((i + 1) % count, i) for i in range(ends)]),
            ],
            axis=dim,
        )
    return cells


def from_root(block, axis, holder):
    block = jnp.where(lax.axis_index(axis) == holder, block, jnp.zeros_like(block))
    return lax.psum(block, axis)


def relax_step(padded, source, coef_pad, weight):
    middle = padded[:, 1:-1]
    coef_mid = coef_pad[:, 1:-1]
    face_north = 0.5 * (coef_mid + coef_pad[:, 2:])
    face_south = 0.5 * (coef_mid + coef_pad[:, :-2])
    face_east = 0.5 * (coef_mid + jnp.roll(coef_mid, -1, 2))
    face_west = 0.5 * (coef_mid + jnp.roll(coef_mid, 1, 2))
    diagonal = 1.0 + face_north + face_south + face_east + face_west
    image = diagonal * middle - face_north * padded[:, 2:] - face_south * padded[:, :-2]
    image = image - face_east * jnp.roll(middle, -1, 2) - face_west * jnp.roll(middle, 1, 2)
    return middle + weight * (source - image) / diagonal


def lookup(zone_ids, diffusivity):
    coefs = jnp.zeros((diffusivity.shape[0],) + zone_ids.shape, jnp.float32)
    for number in range(diffusivity.shape[1]):
        coefs = coefs + jnp.where(
            (zone_ids == number)[None], diffusivity[:, number][:, None, None], jnp.float32(0.0)
        )
    return coefs


def on_device(
    fields,
    zone_ids,
    diffusivity,
    heat_rate,
    weight_in,
    bias_in,
    weight_mid,
    bias_mid,
    weight_out,
    bias_out,
):
    count_here, rows_here, columns = fields.shape
    coefs = lookup(zone_ids, diffusivity)
    stacked = extended(jnp.stack([fields, coefs]), (("space", 2),), 1)
    coef_pad = stacked[1]
    state = relax_step(stacked[0], fields, coef_pad, RELAX_WEIGHTS[0])
    for number in range(1, SWEEPS):
        padded = extended(state, (("space", 1),), 1)
        state = relax_step(padded, fields, coef_pad, RELAX_WEIGHTS[number])
    span = ROWS_BLK * lax.axis_size("field")
    blocks = rows_here * columns // span
    by_block = state.reshape(count_here, blocks, span)

    def one_block(row_block):
        hidden = jax.nn.silu(
            jnp.dot(weight_in, row_block, preferred_element_type=jnp.float32) + bias_in[:, None]
        ).astype(jnp.bfloat16)
        hidden = jax.nn.silu(
            jnp.dot(weight_mid, hidden, preferred_element_type=jnp.float32) + bias_mid[:, None]
        ).astype(jnp.bfloat16)
        return (
            jnp.dot(weight_out, hidden, preferred_element_type=jnp.float32) + bias_out[:, None]
        ).astype(jnp.bfloat16)

    moved = jnp.moveaxis(
        lax.all_to_all(
            by_block.astype(jnp.bfloat16), "field", split_axis=2, concat_axis=0, tiled=True
        ),
        1,
        0,
    )
    change = jnp.moveaxis(lax.map(one_block, moved), 0, 1)
    change = lax.all_to_all(change, "field", split_axis=0, concat_axis=2, tiled=True).astype(
        jnp.float32
    )
    heat_local = by_block[-1] + change[-1]
    heat_new = from_root(heat_local, "field", lax.axis_size("field") - 1)
    first_field = lax.axis_index("field") * count_here
    rate_pad = jnp.concatenate([heat_rate, jnp.zeros((1,), jnp.float32)], 0)
    rate_here = lax.dynamic_slice_in_dim(rate_pad, first_field, count_here)
    factor = jnp.exp(rate_here[:, None, None] * jnp.tanh(heat_new)[None])
    result = by_block + (change * factor).astype(jnp.bfloat16).astype(jnp.float32)
    field_ids = first_field + jnp.arange(count_here, dtype=jnp.int32)
    result = jnp.where((field_ids == FIELDS - 1)[:, None, None], heat_new[None], result)
    return result.reshape(count_here, rows_here, columns)


def solution(mesh):
    return jax.shard_map(
        on_device,
        mesh=mesh,
        in_specs=(
            P("field", "space", None),
            P("space", None),
            P("field", None),
            P(),
            P(),
            P(),
            P(),
            P(),
            P(),
            P(),
        ),
        out_specs=P("field", "space", None),
        check_vma=False,
    )
```

profile of v0, /device:TPU:1, one launch (start us, length us, event | category | flops | bytes accessed | tf_op | source)
XLA Modules:
  0.0 460.7 jit_solution(11899596553922637642)
XLA Ops:
  6.5 1.6 fusion.65
  8.2 6.7 %add_bitcast_fusion = f32[1,1,32,6144]{3,2,1,0:T(8,128)S(1)} fusion(s32[32,6144]{1,0:T(8,128)} %param.13, f32[]{:T(128)} %bitcast.13, f32[]{:T(128)} %bitcast.12, f32[]{:T(128)} %bitcast.11, f32[]{:T(128)} %bitcast.10, f32[]{:T(128)} %bitcast.9, f32[]{:T(128)} %bitcast.8, f32[]{:T(128)} %bitcast.7, f32[]{:T(128)} %bitcast.6), kind=kLoop, calls=%fused_computation.80 | loop fusion | flops 4521984 | bytes 1572896 | tf_op jit(solution)/shard_map/stack | solution.py:70
  14.9 4.8 %collective-permute-start = (f32[2,1,1,6144]{3,2,1,0:T(1,128)S(1)}, f32[2,1,1,6144]{3,2,1,0:T(1,128)S(1)}, u32[]{:S(2)}, u32[]{:S(2)}) collective-permute-start(f32[2,1,1,6144]{3,2,1,0:T(1,128)S(1)} %get-tuple-element.78), channel_id=1, source_target_pairs={{0,16},{16,32},{32,48},{48,64},{64,80},{80,96},{96,112},{112,128},... | collective-permute-start | bytes 147464 | tf_op jit(solution)/shard_map/ppermute | solution.py:20
  19.8 1.3 collective-permute-start.1
  21.1 4.2 collective-permute-done.1
  25.6 0.5 fusion.55
  26.3 1.0 fusion.45
  27.3 0.3 fusion.63
  27.6 1.3 collective-permute-start.2
  28.9 4.6 %collective-permute-start.3 = (f32[1,1,6144]{2,1,0:T(1,128)S(1)}, f32[1,1,6144]{2,1,0:T(1,128)S(1)}, u32[]{:S(2)}, u32[]{:S(2)}) collective-permute-start(f32[1,1,6144]{2,1,0:T(1,128)S(1)} %get-tuple-element.99), channel_id=1, source_target_pairs={{0,16},{16,32},{32,48},{48,64},{64,80},{80,96},{96,112},{112,128},... | collective-permute-start | bytes 73736 | tf_op jit(solution)/shard_map/ppermute | solution.py:20
  33.6 0.9 collective-permute-done.3
  34.4 0.9 fusion.36
  35.3 0.3 fusion.60
  35.6 1.3 collective-permute-start.4
  36.9 6.0 %collective-permute-start.5 = (f32[1,1,6144]{2,1,0:T(1,128)S(1)}, f32[1,1,6144]{2,1,0:T(1,128)S(1)}, u32[]{:S(2)}, u32[]{:S(2)}) collective-permute-start(f32[1,1,6144]{2,1,0:T(1,128)S(1)} %get-tuple-element.89), channel_id=1, source_target_pairs={{0,16},{16,32},{32,48},{48,64},{64,80},{80,96},{96,112},{112,128},... | collective-permute-start | bytes 73736 | tf_op jit(solution)/shard_map/ppermute | solution.py:20
  43.0 0.7 collective-permute-done.5
  43.7 0.9 fusion.51
  44.6 0.6 convert_element_type.50
  45.2 12.8 %copy.13 = bf16[1,12,16384]{1,0,2:T(2,128)(2,1)} copy(bf16[1,12,16384]{2,1,0:T(8,128)(2,1)S(1)} %convert_element_type.50) | data formatting | bytes 786432 | tf_op jit(solution)/shard_map/convert_element_type | solution.py:93
  58.0 0.5 broadcast.69
  58.5 90.8 %reduce = bf16[16384,12]{1,0:T(8,128)(2,1)} reduce(bf16[16384,1,12]{2,1,0:T(2,128)(2,1)} %bitcast.109, bf16[]{:T(256)} %broadcast.69), dimensions={1}, to_apply=%bitcast.85.reduce_sub_computation | reduce | bytes 786434
  149.3 9.5 %reshape.89 = bf16[16,2,6144]{2,1,0:T(2,128)(2,1)} reshape(bf16[16384,12]{1,0:T(8,128)(2,1)} %reduce) | data formatting | bytes 786432
  158.9 13.1 %all-to-all-start = ((bf16[16,2,6144]{2,1,0:T(2,128)(2,1)}), bf16[16,2,6144]{2,1,0:T(2,128)(2,1)S(1)}, u32[]{:S(2)}, u32[]{:S(2)}) async-start(bf16[16,2,6144]{2,1,0:T(2,128)(2,1)} %reshape.89), calls=%async_computation | async-start | bytes 786432 | tf_op jit(solution)/shard_map/all_to_all | solution.py:92
  172.0 12.3 %all-to-all-done = bf16[16,2,6144]{2,1,0:T(2,128)(2,1)S(1)} async-done(((bf16[16,2,6144]{2,1,0:T(2,128)(2,1)}), bf16[16,2,6144]{2,1,0:T(2,128)(2,1)S(1)}, u32[]{:S(2)}, u32[]{:S(2)}) %all-to-all-start) | async-done | bytes 393248 | tf_op jit(solution)/shard_map/all_to_all | solution.py:92
  184.3 12.2 %reshape.90 = bf16[16384,1,12]{2,1,0:T(2,128)(2,1)} reshape(bf16[16,2,6144]{2,1,0:T(2,128)(2,1)S(1)} %all-to-all-done) | data formatting | bytes 786432
  196.5 15.4 %copy.14 = bf16[1,12,16384]{2,1,0:T(8,128)(2,1)S(1)} copy(bf16[1,12,16384]{1,0,2:T(2,128)(2,1)} %bitcast.110) | data formatting | bytes 786432 | tf_op jit(solution)/shard_map/all_to_all | solution.py:92
  212.0 0.3 copy.17
  212.3 0.6 copy-done.1
  212.9 19.7 %while.10 = (s32[]{:T(128)}, bf16[12,16,1024]{2,1,0:T(8,128)(2,1)S(1)}, bf16[12,16,1024]{2,1,0:T(8,128)(2,1)S(1)}, bf16[384,16]{0,1:T(8,128)(2,1)S(1)}, f32[384]...) while((s32[]{:T(128)}, ...), condition=%wide.region_1.2_spmd, body=%wide.region_0.1_spmd.sunk | while | flops 331907072 | bytes 1962605 | solution.py:98
  212.9 0.6 fusion.82
  213.5 1.0 fusion.83
  214.5 0.6 fusion.82
  215.1 1.0 fusion.83
  216.1 0.6 fusion.82
  216.8 1.0 fusion.83
  217.8 0.6 fusion.82
  218.4 1.0 fusion.83
  219.4 0.6 fusion.82
  220.1 1.0 fusion.83
  221.1 0.6 fusion.82
  221.7 1.0 fusion.83
  222.7 0.6 fusion.82
  223.4 1.0 fusion.83
  224.4 0.6 fusion.82
  225.0 1.0 fusion.83
  226.0 0.6 fusion.82
  226.6 1.0 fusion.83
  227.6 0.6 fusion.82
  228.3 1.0 fusion.83
  229.3 0.6 fusion.82
  229.9 1.0 fusion.83
  230.9 0.6 fusion.82
  231.6 1.0 fusion.83
  232.6 1.1 copy.22
  233.6 4.5 all-to-all-start.1
  238.2 0.3 squeeze_reshape.3
  238.5 13.4 %all-to-all-done.1 = bf16[16,12,1024]{2,1,0:T(8,128)(2,1)S(1)} async-done(((bf16[16,12,1024]{2,1,0:T(8,128)(2,1)}), bf16[16,12,1024]{2,1,0:T(8,128)(2,1)S(1)}, u32[]{:S(2)}, u32[]{:S(2)}) %all-to-all-start.1) | async-done | bytes 393248 | tf_op jit(solution)/shard_map/all_to_all | solution.py:99
  252.0 0.5 copy.21
  252.6 0.6 copy.18
  253.3 1.1 add_select_fusion.1
  254.4 0.6 dynamic_slice.7
  255.0 195.6 %all-reduce.2.cloned.1.call-done = f32[12,16384]{1,0:T(8,128)} async-done(((f32[12,16384]{1,0:T(8,128)}), f32[12,16384]{1,0:T(8,128)}) %all-reduce.2.cloned.1.call-update) | async-done | bytes 786448 | tf_op jit(solution)/shard_map/psum | solution.py:31
  450.6 2.2 add_select_fusion
  452.7 1.1 reshape.86
  (33 shorter events, 1.2 us)
Async XLA Ops:
  6.5 8.3 %copy-start = (f32[1,32,6144]{2,1,0:T(8,128)S(1)}, f32[1,32,6144]{2,1,0:T(8,128)}, u32[]{:S(2)}) copy-start(f32[1,32,6144]{2,1,0:T(8,128)} %param.12) | copy-start | bytes 2359300
  14.9 6.1 %collective-permute-start = (f32[2,1,1,6144]{3,2,1,0:T(1,128)S(1)}, f32[2,1,1,6144]{3,2,1,0:T(1,128)S(1)}, u32[]{:S(2)}, u32[]{:S(2)}) collective-permute-start(f32[2,1,1,6144]{3,2,1,0:T(1,128)S(1)} %get-tuple-element.78), channel_id=1, source_target_pairs={{0,16},{16,32},{32,48},{48,64},{64,80},{80,96},{96,112},{112,128},... | collective-permute-start | bytes 147464 | tf_op jit(solution)/shard_map/ppermute | solution.py:20
  19.8 5.5 %collective-permute-start.1 = (f32[2,1,1,6144]{3,2,1,0:T(1,128)S(1)}, f32[2,1,1,6144]{3,2,1,0:T(1,128)S(1)}, u32[]{:S(2)}, u32[]{:S(2)}) collective-permute-start(f32[2,1,1,6144]{3,2,1,0:T(1,128)S(1)} %get-tuple-element.79), channel_id=1, source_target_pairs={{16,0},{32,16},{48,32},{64,48},{80,64},{96,80},{112,96},{128,112},... | collective-permute-start | bytes 147464 | tf_op jit(solution)/shard_map/ppermute | solution.py:22
  27.6 6.0 %collective-permute-start.2 = (f32[1,1,6144]{2,1,0:T(1,128)S(1)}, f32[1,1,6144]{2,1,0:T(1,128)S(1)}, u32[]{:S(2)}, u32[]{:S(2)}) collective-permute-start(f32[1,1,6144]{2,1,0:T(1,128)S(1)} %get-tuple-element.98), channel_id=1, source_target_pairs={{16,0},{32,16},{48,32},{64,48},{80,64},{96,80},{112,96},{128,112},... | collective-permute-start | bytes 73736 | tf_op jit(solution)/shard_map/ppermute | solution.py:22
  28.9 5.6 %collective-permute-start.3 = (f32[1,1,6144]{2,1,0:T(1,128)S(1)}, f32[1,1,6144]{2,1,0:T(1,128)S(1)}, u32[]{:S(2)}, u32[]{:S(2)}) collective-permute-start(f32[1,1,6144]{2,1,0:T(1,128)S(1)} %get-tuple-element.99), channel_id=1, source_target_pairs={{0,16},{16,32},{32,48},{48,64},{64,80},{80,96},{96,112},{112,128},... | collective-permute-start | bytes 73736 | tf_op jit(solution)/shard_map/ppermute | solution.py:20
  35.6 7.4 %collective-permute-start.4 = (f32[1,1,6144]{2,1,0:T(1,128)S(1)}, f32[1,1,6144]{2,1,0:T(1,128)S(1)}, u32[]{:S(2)}, u32[]{:S(2)}) collective-permute-start(f32[1,1,6144]{2,1,0:T(1,128)S(1)} %get-tuple-element.88), channel_id=1, source_target_pairs={{16,0},{32,16},{48,32},{64,48},{80,64},{96,80},{112,96},{128,112},... | collective-permute-start | bytes 73736 | tf_op jit(solution)/shard_map/ppermute | solution.py:22
  36.9 6.8 %collective-permute-start.5 = (f32[1,1,6144]{2,1,0:T(1,128)S(1)}, f32[1,1,6144]{2,1,0:T(1,128)S(1)}, u32[]{:S(2)}, u32[]{:S(2)}) collective-permute-start(f32[1,1,6144]{2,1,0:T(1,128)S(1)} %get-tuple-element.89), channel_id=1, source_target_pairs={{0,16},{16,32},{32,48},{48,64},{64,80},{80,96},{96,112},{112,128},... | collective-permute-start | bytes 73736 | tf_op jit(solution)/shard_map/ppermute | solution.py:20
  158.9 25.4 %all-to-all-start = ((bf16[16,2,6144]{2,1,0:T(2,128)(2,1)}), bf16[16,2,6144]{2,1,0:T(2,128)(2,1)S(1)}, u32[]{:S(2)}, u32[]{:S(2)}) async-start(bf16[16,2,6144]{2,1,0:T(2,128)(2,1)} %reshape.89), calls=%async_computation | async-start | bytes 786432 | tf_op jit(solution)/shard_map/all_to_all | solution.py:92
  211.9 1.0 copy-start.1
  211.9 1.0 copy-start.2
  211.9 0.9 copy-start.3
  211.9 0.9 copy-start.4
  211.9 0.9 copy-start.5
  212.0 0.9 copy-start.6
  233.6 18.3 %all-to-all-start.1 = ((bf16[16,12,1024]{2,1,0:T(8,128)(2,1)}), bf16[16,12,1024]{2,1,0:T(8,128)(2,1)S(1)}, u32[]{:S(2)}, u32[]{:S(2)}) async-start(bf16[16,12,1024]{2,1,0:T(8,128)(2,1)} %bitcast.92), calls=%async_computation.1 | async-start | bytes 1048576 | tf_op jit(solution)/shard_map/all_to_all | solution.py:99
  238.2 212.4 %all-reduce.2.cloned.1.call-start = ((), (), s32[]{:S(2)}) async-start(), calls=%async_computation.2 | async-start | bytes 2097152 | tf_op jit(solution)/shard_map/psum | solution.py:31
  253.2 1.1 copy-start.7
Sparse Core Ops, SparseCore 0:
  254.5 196.0 all-reduce.1
where the time goes:
time: 462 us; the launch traced here: 461 us
  waiting for transfers between devices  227 us (49%)
  other arithmetic  104 us (23%)
  local copies, waits for them, and re-layouts  59.4 us (13%)
  starting transfers between devices  37 us (8%)
  matrix products  19.6 us (4%)
  between operations  13.7 us (3%)
    psum x1, waiting for transfers between devices, from_root(): return lax.psum(block, axis)  196 us
    unnamed x1, other arithmetic  90.8 us
    unnamed x22, local copies, waits for them, and re-layouts  23.9 us
    ppermute x3, starting transfers between devices, extended(): lax.ppermute(tail, axis, [(i, (i + 1) % count) for i in range(ends)])  15.5 us
    all_to_all x1, local copies, waits for them, and re-layouts, on_device(): lax.all_to_all(by_block.astype(jnp.bfloat16), 'field', split_axis=2, conc...  15.4 us
    all_to_all x1, waiting for transfers between devices, on_device(): lax.all_to_all(change, 'field', split_axis=0, concat_axis=2, tiled=True)  13.4 us
    convert_element_type x2, local copies, waits for them, and re-layouts, on_device(): by_block.astype(jnp.bfloat16)  13.4 us
    all_to_all x1, starting transfers between devices, on_device(): lax.all_to_all(by_block.astype(jnp.bfloat16), 'field', split_axis=2, conc...  13.1 us
  transfers between devices with their start and end apart: 9, of which 6 were waited for; matrix products, arithmetic and copies ran while one was open for 0% of the time, Pallas kernels for 0%

commit v1 on v0

--- a/solution.py
+++ b/solution.py
@@ -89,8 +89,14 @@
         ).astype(jnp.bfloat16)
 
     moved = jnp.moveaxis(
-        lax.all_to_all(
-            by_block.astype(jnp.bfloat16), "field", split_axis=2, concat_axis=0, tiled=True
+        jnp.concatenate(
+            lax.all_to_all(
+                jnp.stack(jnp.split(by_block.astype(jnp.bfloat16), lax.axis_size("field"), axis=2)),
+                "field",
+                0,
+                0,
+            ),
+            axis=0,
         ),
         1,
         0,

time: 462 us -> 330 us (0.71)
  other arithmetic: 104 us -> 13.2 us
  local copies, waits for them, and re-layouts: 59.4 us -> 18.1 us
    unnamed x1 -> x0, other arithmetic: 90.8 us -> none
    all_to_all x1 -> x0, local copies, waits for them, and re-layouts: 15.4 us -> none  [on_device(): lax.all_to_all(by_block.astype(jnp.bfloat16), 'field', split_axis=2, conc...]
    unnamed x22 -> x33, local copies, waits for them, and re-layouts: 23.9 us -> 10 us
    convert_element_type x2 -> x1, local copies, waits for them, and re-layouts: 13.4 us -> 0.59 us  [on_device(): by_block.astype(jnp.bfloat16)]
where the time goes in v1:
time: 330 us
  waiting for transfers between devices  228 us (69%)
  starting transfers between devices  36.8 us (11%)
  matrix products  19.5 us (6%)
  local copies, waits for them, and re-layouts  18.1 us (5%)
  between operations  13.7 us (4%)
  other arithmetic  13.2 us (4%)
    psum x1, waiting for transfers between devices, from_root(): return lax.psum(block, axis)  195 us
    ppermute x3, starting transfers between devices, extended(): lax.ppermute(tail, axis, [(i, (i + 1) % count) for i in range(ends)])  15.3 us
    all_to_all x1, waiting for transfers between devices, on_device(): lax.all_to_all(jnp.stack(jnp.split(by_block.astype(jnp.bfloat16), lax.axi...  13.7 us
    all_to_all x1, waiting for transfers between devices, on_device(): lax.all_to_all(change, 'field', split_axis=0, concat_axis=2, tiled=True)  13.4 us
    all_to_all x1, starting transfers between devices, on_device(): lax.all_to_all(jnp.stack(jnp.split(by_block.astype(jnp.bfloat16), lax.axi...  13.1 us
    dot_general x12, matrix products, one_block(): jnp.dot(weight_out, hidden, preferred_element_type=jnp.float32)  11.9 us
    unnamed x33, local copies, waits for them, and re-layouts  10 us
    dot_general x12, matrix products, one_block(): jnp.dot(weight_in, row_block, preferred_element_type=jnp.float32)  7.57 us
  transfers between devices with their start and end apart: 9, of which 6 were waited for; matrix products, arithmetic and copies ran while one was open for 0% of the time, Pallas kernels for 0%

profile of v1, /device:TPU:1, one launch (start us, length us, event | category | flops | bytes accessed | tf_op | source)
XLA Modules:
  0.0 329.8 jit_solution(1656951999660638402)
XLA Ops:
  6.5 1.6 fusion.65
  8.2 6.6 %add_bitcast_fusion = f32[1,1,32,6144]{3,2,1,0:T(8,128)S(1)} fusion(s32[32,6144]{1,0:T(8,128)} %param.13, f32[]{:T(128)} %bitcast.13, f32[]{:T(128)} %bitcast.12, f32[]{:T(128)} %bitcast.11, f32[]{:T(128)} %bitcast.10, f32[]{:T(128)} %bitcast.9, f32[]{:T(128)} %bitcast.8, f32[]{:T(128)} %bitcast.7, f32[]{:T(128)} %bitcast.6), kind=kLoop, calls=%fused_computation.80 | loop fusion | flops 4521984 | bytes 1572896 | tf_op jit(solution)/shard_map/stack | solution.py:70
  14.9 4.8 %collective-permute-start = (f32[2,1,1,6144]{3,2,1,0:T(1,128)S(1)}, f32[2,1,1,6144]{3,2,1,0:T(1,128)S(1)}, u32[]{:S(2)}, u32[]{:S(2)}) collective-permute-start(f32[2,1,1,6144]{3,2,1,0:T(1,128)S(1)} %get-tuple-element.105), channel_id=1, source_target_pairs={{0,16},{16,32},{32,48},{48,64},{64,80},{80,96},{96,112},{112,128},... | collective-permute-start | bytes 147464 | tf_op jit(solution)/shard_map/ppermute | solution.py:20
  19.7 1.3 collective-permute-start.1
  21.0 4.2 %collective-permute-done.1 = f32[2,1,1,6144]{3,2,1,0:T(1,128)S(1)} collective-permute-done((f32[2,1,1,6144]{3,2,1,0:T(1,128)S(1)}, f32[2,1,1,6144]{3,2,1,0:T(1,128)S(1)}, u32[]{:S(2)}, u32[]{:S(2)}) %collective-permute-start.1) | collective-permute-done | bytes 49184 | tf_op jit(solution)/shard_map/ppermute | solution.py:22
  26.2 1.0 fusion.45
  27.6 1.3 collective-permute-start.2
  28.9 4.6 %collective-permute-start.3 = (f32[1,1,6144]{2,1,0:T(1,128)S(1)}, f32[1,1,6144]{2,1,0:T(1,128)S(1)}, u32[]{:S(2)}, u32[]{:S(2)}) collective-permute-start(f32[1,1,6144]{2,1,0:T(1,128)S(1)} %get-tuple-element.126), channel_id=1, source_target_pairs={{0,16},{16,32},{32,48},{48,64},{64,80},{80,96},{96,112},{112,128},... | collective-permute-start | bytes 73736 | tf_op jit(solution)/shard_map/ppermute | solution.py:20
  33.6 0.9 collective-permute-done.3
  34.4 0.9 fusion.36
  35.6 1.3 collective-permute-start.4
  36.9 5.8 %collective-permute-start.5 = (f32[1,1,6144]{2,1,0:T(1,128)S(1)}, f32[1,1,6144]{2,1,0:T(1,128)S(1)}, u32[]{:S(2)}, u32[]{:S(2)}) collective-permute-start(f32[1,1,6144]{2,1,0:T(1,128)S(1)} %get-tuple-element.116), channel_id=1, source_target_pairs={{0,16},{16,32},{32,48},{48,64},{64,80},{80,96},{96,112},{112,128},... | collective-permute-start | bytes 73736 | tf_op jit(solution)/shard_map/ppermute | solution.py:20
  42.8 0.9 collective-permute-done.5
  43.7 0.9 fusion.51
  45.3 0.6 constant_dynamic-update-slice_fusion.15
  45.9 0.6 constant_dynamic-update-slice_fusion.14
  46.5 0.6 constant_dynamic-update-slice_fusion.13
  47.1 0.6 constant_dynamic-update-slice_fusion.12
  47.7 0.6 constant_dynamic-update-slice_fusion.11
  48.4 0.6 constant_dynamic-update-slice_fusion.10
  49.0 0.6 constant_dynamic-update-slice_fusion.9
  49.6 0.6 constant_dynamic-update-slice_fusion.8
  50.2 0.6 constant_dynamic-update-slice_fusion.7
  50.8 0.6 constant_dynamic-update-slice_fusion.6
  51.4 0.6 constant_dynamic-update-slice_fusion.5
  52.1 0.6 constant_dynamic-update-slice_fusion.4
  52.7 0.6 constant_dynamic-update-slice_fusion.3
  53.3 0.6 constant_dynamic-update-slice_fusion.2
  53.9 0.6 constant_dynamic-update-slice_fusion.1
  54.5 0.6 constant_dynamic-update-slice_fusion
  55.1 13.1 %all-to-all-start = ((bf16[16,1,12,1024]{3,2,1,0:T(8,128)(2,1)}), bf16[16,1,12,1024]{3,2,1,0:T(8,128)(2,1)S(1)}, u32[]{:S(2)}, u32[]{:S(2)}) async-start(bf16[16,1,12,1024]{3,2,1,0:T(8,128)(2,1)} %constant_dynamic-update-slice_fusion), calls=%async_computation | async-start | bytes 1048576 | tf_op jit(solution)/shard_map/all_to_all | solution.py:93
  68.2 13.7 %all-to-all-done = bf16[16,1,12,1024]{3,2,1,0:T(8,128)(2,1)S(1)} async-done(((bf16[16,1,12,1024]{3,2,1,0:T(8,128)(2,1)}), bf16[16,1,12,1024]{3,2,1,0:T(8,128)(2,1)S(1)}, u32[]{:S(2)}, u32[]{:S(2)}) %all-to-all-start) | async-done | bytes 393248 | tf_op jit(solution)/shard_map/all_to_all | solution.py:93
  82.2 19.6 %while.10 = (s32[]{:T(128)}, bf16[12,16,1024]{2,1,0:T(8,128)(2,1)S(1)}, bf16[12,16,1024]{2,1,0:T(8,128)(2,1)S(1)}, bf16[384,16]{0,1:T(8,128)(2,1)S(1)}, f32[384]...) while((s32[]{:T(128)}, ...), condition=%wide.region_1.2_spmd, body=%wide.region_0.1_spmd.sunk | while | flops 331907072 | bytes 1962605 | solution.py:104
  82.9 1.0 fusion.83
  83.8 0.6 fusion.82
  84.5 1.0 fusion.83
  85.5 0.6 fusion.82
  86.1 1.0 fusion.83
  87.1 0.6 fusion.82
  87.8 1.0 fusion.83
  88.7 0.6 fusion.82
  89.4 1.0 fusion.83
  90.4 0.6 fusion.82
  91.0 1.0 fusion.83
  92.0 0.6 fusion.82
  92.7 1.0 fusion.83
  93.6 0.6 fusion.82
  94.3 1.0 fusion.83
  95.3 0.6 fusion.82
  95.9 1.0 fusion.83
  96.9 0.6 fusion.82
  97.6 1.0 fusion.83
  98.5 0.6 fusion.82
  99.2 1.0 fusion.83
  100.2 0.6 fusion.82
  100.8 1.0 fusion.83
  101.8 1.1 copy.36
  102.9 4.5 %all-to-all-start.1 = ((bf16[16,12,1024]{2,1,0:T(8,128)(2,1)}), bf16[16,12,1024]{2,1,0:T(8,128)(2,1)S(1)}, u32[]{:S(2)}, u32[]{:S(2)}) async-start(bf16[16,12,1024]{2,1,0:T(8,128)(2,1)} %bitcast.145), calls=%async_computation.1 | async-start | bytes 1048576 | tf_op jit(solution)/shard_map/all_to_all | solution.py:105
  107.8 13.4 %all-to-all-done.1 = bf16[16,12,1024]{2,1,0:T(8,128)(2,1)S(1)} async-done(((bf16[16,12,1024]{2,1,0:T(8,128)(2,1)}), bf16[16,12,1024]{2,1,0:T(8,128)(2,1)S(1)}, u32[]{:S(2)}, u32[]{:S(2)}) %all-to-all-start.1) | async-done | bytes 393248 | tf_op jit(solution)/shard_map/all_to_all | solution.py:105
  121.9 0.6 copy.32
  122.5 1.1 add_select_fusion.1
  124.3 195.4 %all-reduce.2.cloned.1.call-done = f32[12,16384]{1,0:T(8,128)} async-done(((f32[12,16384]{1,0:T(8,128)}), f32[12,16384]{1,0:T(8,128)}) %all-reduce.2.cloned.1.call-update) | async-done | bytes 786448 | tf_op jit(solution)/shard_map/psum | solution.py:31
  319.7 2.2 add_select_fusion
  321.9 1.1 reshape.90
  (42 shorter events, 5.0 us)
Async XLA Ops:
  6.5 8.3 %copy-start = (f32[1,32,6144]{2,1,0:T(8,128)S(1)}, f32[1,32,6144]{2,1,0:T(8,128)}, u32[]{:S(2)}) copy-start(f32[1,32,6144]{2,1,0:T(8,128)} %param.12) | copy-start | bytes 2359300
  14.9 6.1 %collective-permute-start = (f32[2,1,1,6144]{3,2,1,0:T(1,128)S(1)}, f32[2,1,1,6144]{3,2,1,0:T(1,128)S(1)}, u32[]{:S(2)}, u32[]{:S(2)}) collective-permute-start(f32[2,1,1,6144]{3,2,1,0:T(1,128)S(1)} %get-tuple-element.105), channel_id=1, source_target_pairs={{0,16},{16,32},{32,48},{48,64},{64,80},{80,96},{96,112},{112,128},... | collective-permute-start | bytes 147464 | tf_op jit(solution)/shard_map/ppermute | solution.py:20
  19.7 5.5 %collective-permute-start.1 = (f32[2,1,1,6144]{3,2,1,0:T(1,128)S(1)}, f32[2,1,1,6144]{3,2,1,0:T(1,128)S(1)}, u32[]{:S(2)}, u32[]{:S(2)}) collective-permute-start(f32[2,1,1,6144]{3,2,1,0:T(1,128)S(1)} %get-tuple-element.106), channel_id=1, source_target_pairs={{16,0},{32,16},{48,32},{64,48},{80,64},{96,80},{112,96},{128,112},... | collective-permute-start | bytes 147464 | tf_op jit(solution)/shard_map/ppermute | solution.py:22
  27.6 6.0 %collective-permute-start.2 = (f32[1,1,6144]{2,1,0:T(1,128)S(1)}, f32[1,1,6144]{2,1,0:T(1,128)S(1)}, u32[]{:S(2)}, u32[]{:S(2)}) collective-permute-start(f32[1,1,6144]{2,1,0:T(1,128)S(1)} %get-tuple-element.125), channel_id=1, source_target_pairs={{16,0},{32,16},{48,32},{64,48},{80,64},{96,80},{112,96},{128,112},... | collective-permute-start | bytes 73736 | tf_op jit(solution)/shard_map/ppermute | solution.py:22
  28.9 5.6 %collective-permute-start.3 = (f32[1,1,6144]{2,1,0:T(1,128)S(1)}, f32[1,1,6144]{2,1,0:T(1,128)S(1)}, u32[]{:S(2)}, u32[]{:S(2)}) collective-permute-start(f32[1,1,6144]{2,1,0:T(1,128)S(1)} %get-tuple-element.126), channel_id=1, source_target_pairs={{0,16},{16,32},{32,48},{48,64},{64,80},{80,96},{96,112},{112,128},... | collective-permute-start | bytes 73736 | tf_op jit(solution)/shard_map/ppermute | solution.py:20
  35.6 7.2 %collective-permute-start.4 = (f32[1,1,6144]{2,1,0:T(1,128)S(1)}, f32[1,1,6144]{2,1,0:T(1,128)S(1)}, u32[]{:S(2)}, u32[]{:S(2)}) collective-permute-start(f32[1,1,6144]{2,1,0:T(1,128)S(1)} %get-tuple-element.115), channel_id=1, source_target_pairs={{16,0},{32,16},{48,32},{64,48},{80,64},{96,80},{112,96},{128,112},... | collective-permute-start | bytes 73736 | tf_op jit(solution)/shard_map/ppermute | solution.py:22
  36.9 6.8 %collective-permute-start.5 = (f32[1,1,6144]{2,1,0:T(1,128)S(1)}, f32[1,1,6144]{2,1,0:T(1,128)S(1)}, u32[]{:S(2)}, u32[]{:S(2)}) collective-permute-start(f32[1,1,6144]{2,1,0:T(1,128)S(1)} %get-tuple-element.116), channel_id=1, source_target_pairs={{0,16},{16,32},{32,48},{48,64},{64,80},{80,96},{96,112},{112,128},... | collective-permute-start | bytes 73736 | tf_op jit(solution)/shard_map/ppermute | solution.py:20
  45.2 37.0 %copy-start.1 = (bf16[384,384]{1,0:T(8,128)(2,1)S(1)}, bf16[384,384]{1,0:T(8,128)(2,1)}, u32[]{:S(2)}) copy-start(bf16[384,384]{1,0:T(8,128)(2,1)} %param.18) | copy-start | bytes 884740
  45.2 37.0 %copy-start.2 = (bf16[384,16]{0,1:T(8,128)(2,1)S(1)}, bf16[384,16]{0,1:T(8,128)(2,1)}, u32[]{:S(2)}) copy-start(bf16[384,16]{0,1:T(8,128)(2,1)} %param.16) | copy-start | bytes 36868
  45.2 37.0 %copy-start.3 = (bf16[16,384]{1,0:T(8,128)(2,1)S(1)}, bf16[16,384]{1,0:T(8,128)(2,1)}, u32[]{:S(2)}) copy-start(bf16[16,384]{1,0:T(8,128)(2,1)} %param.20) | copy-start | bytes 36868
  45.2 37.0 %copy-start.4 = (f32[384]{0:T(512)S(1)}, f32[384]{0:T(512)}, u32[]{:S(2)}) copy-start(f32[384]{0:T(512)} %param.17) | copy-start | bytes 4612
  45.2 37.0 %copy-start.5 = (f32[384]{0:T(512)S(1)}, f32[384]{0:T(512)}, u32[]{:S(2)}) copy-start(f32[384]{0:T(512)} %param.19) | copy-start | bytes 4612
  45.2 37.0 %copy-start.6 = (f32[16]{0:T(128)S(1)}, f32[16]{0:T(128)}, u32[]{:S(2)}) copy-start(f32[16]{0:T(128)} %param.21) | copy-start | bytes 196
  55.1 26.8 %all-to-all-start = ((bf16[16,1,12,1024]{3,2,1,0:T(8,128)(2,1)}), bf16[16,1,12,1024]{3,2,1,0:T(8,128)(2,1)S(1)}, u32[]{:S(2)}, u32[]{:S(2)}) async-start(bf16[16,1,12,1024]{3,2,1,0:T(8,128)(2,1)} %constant_dynamic-update-slice_fusion), calls=%async_computation | async-start | bytes 1048576 | tf_op jit(solution)/shard_map/all_to_all | solution.py:93
  102.9 18.3 %all-to-all-start.1 = ((bf16[16,12,1024]{2,1,0:T(8,128)(2,1)}), bf16[16,12,1024]{2,1,0:T(8,128)(2,1)S(1)}, u32[]{:S(2)}, u32[]{:S(2)}) async-start(bf16[16,12,1024]{2,1,0:T(8,128)(2,1)} %bitcast.145), calls=%async_computation.1 | async-start | bytes 1048576 | tf_op jit(solution)/shard_map/all_to_all | solution.py:105
  107.4 212.3 %all-reduce.2.cloned.1.call-start = ((), (), s32[]{:S(2)}) async-start(), calls=%async_computation.2 | async-start | bytes 2097152 | tf_op jit(solution)/shard_map/psum | solution.py:31
  122.5 1.1 copy-start.7
Sparse Core Ops, SparseCore 0:
  123.7 195.9 all-reduce.1
